TPU v7x, 128 devices: a whole 4x4x4 slice. The times are simulated.
128 devices in a mesh: dp: 16 (over y, x_lo, core), ctx: 8 (over z, x_hi).
Axes of the slice: x: 4 (x_hi: 2, x_lo: 2; x = x_hi * 2 + x_lo), y: 4, z: 4, core: 2. Of those that a mesh axis runs over, the one named last changes fastest.
Arguments:
- query_in: bfloat16 [32768, 2048], P(('dp', 'ctx')), may hold values from -16 to 16
- key_in: bfloat16 [32768, 512], P(('dp', 'ctx')), may hold values from -16 to 16
- value_in: bfloat16 [32768, 512], P(('dp', 'ctx')), may hold values from -6 to 6
- grad_out: bfloat16 [32768, 2048], P(('dp', 'ctx')), may hold values from -6 to 6
- target: int32 [32768], P(('dp', 'ctx')), may hold values from 0 to 32767, as said below
- span_order: int32 [16, 16], P('dp'), may hold values from 0 to 15, each once within a row
- doc_ids: int32 [16, 2048], P('dp', 'ctx'), may hold values from 0 to 7, never falling along the last dimension, each value on 1 to 1024 neighbouring positions
Outputs:
- grad_query: float32 [32768, 2048], P(('dp', 'ctx'))
- grad_key: float32 [32768, 512], P(('dp', 'ctx'))
- grad_value: float32 [32768, 512], P(('dp', 'ctx'))
Inputs may be any that keep to these rules, and one draw needn't show every extreme that they name: target is a permutation of the 32768 packed rows; of the 256 rows of one device at most 4 go to any one block of 256 packed rows, and exactly 4 go to some block. `span_order`: each row names every span once. `doc_ids`: each document is one run of 1 to 1024 positions; numbers never fall along a pack.
All inputs are finite; a program needn't handle non-finite values.
Results may differ from a plain program's by a relative error of at most 0.035.
Values may be sent and summed in bfloat16 or wider, within the bound.
No kernel may reach another device: no remote copies, remote signals or barrier semaphores. Data moves between devices by JAX's collectives and lax.ppermute only.
A program may use at most 128 MiB of HBM per device.

v0:
```python
import jax
import jax.numpy as jnp
from jax import lax
from jax.sharding import PartitionSpec as P

HQ = 16
HK = 4
DH = 128
block_keys = 512


def visible(query_pos, query_doc, key_pos, key_doc):
    return (key_pos[None, :] <= query_pos[:, None]) & (key_doc[None, :] == query_doc[:, None])


def masked_scores(query_blk, key_blk, allowed):
    raw_scores = jnp.einsum(
        "qhgd,khd->hgqk", query_blk, key_blk, preferred_element_type=jnp.float32
    ) * DH ** (-0.5)
    return jnp.where(allowed[None, None], raw_scores, -jnp.inf)


def grad_terms(query_blk, grad_blk, lse_blk, delta_blk, key_blk, value_blk, allowed):
    scores = masked_scores(query_blk, key_blk, allowed)
    probs = jnp.exp(scores - lse_blk[..., None])
    probs_low = probs.astype(jnp.bfloat16)
    dprobs = jnp.einsum("qhgd,khd->hgqk", grad_blk, value_blk, preferred_element_type=jnp.float32)
    dscore_low = (probs * (dprobs - delta_blk[..., None])).astype(jnp.bfloat16)
    return (probs_low, dscore_low)


def local(query_in, key_in, value_in, grad_out, target, span_order, doc_ids):
    local_rows = query_in.shape[0]
    devices = lax.axis_size(("dp", "ctx"))
    ctx_size = lax.axis_size("ctx")
    capacity = local_rows // devices + 2
    groups = HQ // HK
    score_scale = DH ** (-0.5)
    q_cols = query_in.shape[1]
    k_cols = key_in.shape[1]
    owners = target // local_rows
    onehot = (owners[:, None] == jnp.arange(devices, dtype=jnp.int32)[None, :]).astype(jnp.int32)
    earlier = jnp.cumsum(onehot, axis=0) - onehot
    slot_ids = owners * capacity + jnp.sum(earlier * onehot, axis=1)
    place_col = (
        jnp.zeros((local_rows, 128), jnp.bfloat16)
        .at[:, 0]
        .set((target % local_rows + 1).astype(jnp.bfloat16))
    )
    payload = jnp.concatenate([query_in, key_in, value_in, grad_out, place_col], axis=1)
    width = payload.shape[1]
    holder = jnp.zeros((devices * capacity, width), jnp.bfloat16).at[slot_ids].set(payload)
    got = lax.all_to_all(
        holder.reshape(devices, capacity, width),
        ("dp", "ctx"),
        split_axis=0,
        concat_axis=0,
        tiled=True,
    ).reshape(devices * capacity, width)
    arrived = got[:, 2 * q_cols + 2 * k_cols].astype(jnp.int32) - 1
    landing = jnp.where(arrived >= 0, arrived, local_rows)
    rows = jnp.zeros((local_rows, width), jnp.bfloat16).at[landing].set(got, mode="drop")
    query = rows[:, :q_cols]
    kv_rows = rows[:, q_cols : q_cols + 2 * k_cols]
    grad_rows = rows[:, q_cols + 2 * k_cols : 2 * q_cols + 2 * k_cols]
    span_rows = local_rows // 2
    span_seq = span_order[0]
    pack_len = local_rows * ctx_size
    positions = (
        span_seq[:, None] * span_rows + jnp.arange(span_rows, dtype=jnp.int32)[None, :]
    ).reshape(-1)
    ctx_index = lax.axis_index("ctx")
    own_pos = lax.dynamic_slice_in_dim(positions, ctx_index * local_rows, local_rows)
    doc_col = (
        jnp.zeros((local_rows, 128), jnp.bfloat16).at[:, 0].set(doc_ids[0].astype(jnp.bfloat16))
    )
    gathered = lax.all_gather(
        jnp.concatenate([kv_rows, doc_col], axis=1), "ctx", axis=0, tiled=True
    )
    seq_docs = gathered[:, 2 * k_cols].astype(jnp.int32)
    doc_all = seq_docs.reshape(2 * ctx_size, span_rows)[span_seq].reshape(-1)
    own_docs = lax.dynamic_slice_in_dim(doc_all, ctx_index * local_rows, local_rows)
    query_heads = query.reshape(local_rows, HK, groups, DH)
    grad_heads = grad_rows.reshape(local_rows, HK, groups, DH)
    key_heads = gathered[:, :k_cols].reshape(pack_len, HK, DH)
    value_heads = gathered[:, k_cols : 2 * k_cols].reshape(pack_len, HK, DH)
    num_blocks = pack_len // block_keys

    def key_block(block_index):
        first_key = block_index * block_keys
        return (
            lax.dynamic_slice_in_dim(key_heads, first_key, block_keys),
            lax.dynamic_slice_in_dim(value_heads, first_key, block_keys),
            lax.dynamic_slice_in_dim(positions, first_key, block_keys),
            lax.dynamic_slice_in_dim(doc_all, first_key, block_keys),
        )

    def stats_step(block_index, carry):
        key_blk, value_blk, key_pos, key_doc = key_block(block_index)
        allowed = visible(own_pos, own_docs, key_pos, key_doc)
        running_max, running_sum = carry
        scores = masked_scores(query_heads, key_blk, allowed)
        new_max = jnp.maximum(running_max, jnp.max(scores, axis=-1))
        rescale = jnp.exp(running_max - new_max)
        running_sum = running_sum * rescale + jnp.sum(jnp.exp(scores - new_max[..., None]), axis=-1)
        return (new_max, running_sum)

    start_stats = (
        jnp.full((HK, groups, local_rows), -1e30, jnp.float32),
        jnp.zeros((HK, groups, local_rows), jnp.float32),
    )
    running_max, running_sum = lax.fori_loop(0, num_blocks, stats_step, start_stats)
    log_norm = running_max + jnp.log(running_sum)

    def output_step(block_index, carry):
        key_blk, value_blk, key_pos, key_doc = key_block(block_index)
        allowed = visible(own_pos, own_docs, key_pos, key_doc)
        scores = masked_scores(query_heads, key_blk, allowed)
        probs_low = jnp.exp(scores - log_norm[..., None]).astype(jnp.bfloat16)
        return carry + jnp.einsum(
            "hgqk,khd->qhgd", probs_low, value_blk, preferred_element_type=jnp.float32
        )

    summed = lax.fori_loop(
        0, num_blocks, output_step, jnp.zeros((local_rows, HK, groups, DH), jnp.float32)
    )
    attended_low = summed.astype(jnp.bfloat16)
    delta = jnp.sum(
        grad_heads.astype(jnp.float32) * attended_low.astype(jnp.float32), axis=-1
    ).transpose(1, 2, 0)

    def back_step(block_index, carry):
        key_blk, value_blk, key_pos, key_doc = key_block(block_index)
        allowed = visible(own_pos, own_docs, key_pos, key_doc)
        dquery, dkey_all, dvalue_all = carry
        probs_low, dscore_low = grad_terms(
            query_heads, grad_heads, log_norm, delta, key_blk, value_blk, allowed
        )
        dquery = dquery + jnp.einsum(
            "hgqk,khd->qhgd", dscore_low, key_blk, preferred_element_type=jnp.float32
        )
        dkey = (
            jnp.einsum(
                "hgqk,qhgd->khd", dscore_low, query_heads, preferred_element_type=jnp.float32
            )
            * score_scale
        )
        dvalue = jnp.einsum(
            "hgqk,qhgd->khd", probs_low, grad_heads, preferred_element_type=jnp.float32
        )
        first_key = block_index * block_keys
        dkey_all = lax.dynamic_update_slice_in_dim(
            dkey_all, dkey.reshape(block_keys, HK * DH), first_key, 0
        )
        dvalue_all = lax.dynamic_update_slice_in_dim(
            dvalue_all, dvalue.reshape(block_keys, HK * DH), first_key, 0
        )
        return (dquery, dkey_all, dvalue_all)

    start_back = (
        jnp.zeros((local_rows, HK, groups, DH), jnp.float32),
        jnp.zeros((pack_len, HK * DH), jnp.float32),
        jnp.zeros((pack_len, HK * DH), jnp.float32),
    )
    dquery, dkey_all, dvalue_all = lax.fori_loop(0, num_blocks, back_step, start_back)
    partial = jnp.concatenate([dkey_all, dvalue_all], axis=1).astype(jnp.bfloat16)
    summed_kv = jnp.sum(
        lax.all_to_all(
            partial.reshape(ctx_size, local_rows, 2 * k_cols),
            "ctx",
            split_axis=0,
            concat_axis=0,
            tiled=True,
        ).astype(jnp.float32),
        axis=0,
    )
    dquery_full = (dquery * score_scale).reshape(local_rows, HQ * DH)
    source_rows = jnp.where(arrived >= 0, arrived, 0)
    result = jnp.concatenate(
        [dquery_full.astype(jnp.bfloat16), summed_kv.astype(jnp.bfloat16)], axis=1
    )
    back = (
        lax.all_to_all(
            result[source_rows].reshape(devices, capacity, q_cols + 2 * k_cols),
            ("dp", "ctx"),
            split_axis=0,
            concat_axis=0,
            tiled=True,
        )
        .reshape(devices * capacity, q_cols + 2 * k_cols)[slot_ids]
        .astype(jnp.float32)
    )
    return (back[:, :q_cols], back[:, q_cols : q_cols + k_cols], back[:, q_cols + k_cols :])


def solution(mesh):
    placed = (
        P(("dp", "ctx"), None),
        P(("dp", "ctx"), None),
        P(("dp", "ctx"), None),
        P(("dp", "ctx"), None),
        P(("dp", "ctx")),
        P("dp", None),
        P("dp", "ctx"),
    )
    return jax.shard_map(
        local,
        mesh=mesh,
        in_specs=placed,
        out_specs=(P(("dp", "ctx"), None), P(("dp", "ctx"), None), P(("dp", "ctx"), None)),
        check_vma=False,
    )
```

profile of v0, /device:TPU:1, one launch (start us, length us, event | category | flops | bytes accessed | tf_op | source)
XLA Modules:
  0.0 499.3 jit_solution(9435614256057329827)
XLA Ops:
  11.9 2.4 constant_dynamic-update-slice_fusion.5
  17.6 8.6 %scatter_custom_fusion = bf16[512,5248]{1,0:T(8,128)(2,1)} fusion(s32[256]{0:T(256)S(1)} %compare_select_fusion.4, bf16[256,5248]{1,0:T(8,128)(2,1)} %pad_dynamic-update-slice_fusion, bf16[]{:T(256)} %constant.226.clone.1), kind=kCustom, calls=%fused_computation.63 | custom fusion | bytes 5374464 | tf_op jit(solution)/shard_map/scatter | solution.py:52
  26.2 9.4 %reshape.352 = bf16[128,4,5248]{2,1,0:T(4,128)(2,1)} reshape(bf16[512,5248]{1,0:T(8,128)(2,1)} %scatter_custom_fusion) | data formatting | bytes 10747904 | tf_op jit(solution)/shard_map/reshape | solution.py:54
  35.6 11.9 %all-to-all-start = ((bf16[128,4,5248]{2,1,0:T(4,128)(2,1)}), bf16[128,4,5248]{2,1,0:T(4,128)(2,1)}, u32[]{:S(2)}, u32[]{:S(2)}) async-start(bf16[128,4,5248]{2,1,0:T(4,128)(2,1)} %reshape.352), calls=%async_computation | async-start | bytes 10747904 | tf_op jit(solution)/shard_map/all_to_all | solution.py:53
  48.9 64.2 %all-to-all-done = bf16[128,4,5248]{2,1,0:T(4,128)(2,1)} async-done(((bf16[128,4,5248]{2,1,0:T(4,128)(2,1)}), bf16[128,4,5248]{2,1,0:T(4,128)(2,1)}, u32[]{:S(2)}, u32[]{:S(2)}) %all-to-all-start) | async-done | bytes 5373984 | tf_op jit(solution)/shard_map/all_to_all | solution.py:53
  113.1 9.0 %reshape.399 = bf16[512,5248]{1,0:T(8,128)(2,1)} reshape(bf16[128,4,5248]{2,1,0:T(4,128)(2,1)} %all-to-all-done) | data formatting | bytes 10747904 | tf_op jit(solution)/shard_map/reshape | solution.py:59
  122.1 1.7 fusion.57
  123.9 10.3 %scatter_custom_fusion.1 = bf16[256,5248]{1,0:T(8,128)(2,1)S(1)} fusion(s32[512]{0:T(512)S(1)} %get-tuple-element.848, bf16[512,5248]{1,0:T(8,128)(2,1)} %reshape.399, bf16[]{:T(256)} %constant.226.clone.1), kind=kCustom, calls=%fused_computation.68 | custom fusion | bytes 2687488 | tf_op jit(solution)/shard_map/scatter | solution.py:62
  136.1 2.7 fusion.68
  142.0 2.4 copy.108
  144.4 2.3 copy.134
  146.7 59.6 %all-gather.2.cloned.1.call-done = bf16[2048,1152]{1,0:T(8,128)(2,1)} async-done(((bf16[256,1152]{1,0:T(8,128)(2,1)}), bf16[2048,1152]{1,0:T(8,128)(2,1)}) %all-gather.2.cloned.1.call-update) | async-done | bytes 4718608 | tf_op jit(solution)/shard_map/all_gather | solution.py:77
  206.3 4.5 fusion.67
  210.9 4.0 copy.103
  216.9 4.0 copy.100
  220.8 3.9 copy.107
  224.8 18.0 %while.50 = (s32[]{:T(128)}, f32[4,4,256]{2,1,0:T(4,128)S(1)}, f32[4,4,256]{2,1,0:T(4,128)S(1)}, s32[2048]{0:T(1024)S(1)}, s32[256]{0:T(256)S(1)}, /*index=5*/s3...) while((s32[]{:T(128)}, f32[4,4,256]{2,1,0:T(4,128)S(1)}, ...), condition=%wide.region_9.10_spmd.clone, body=%wide.region_6.9_spmd.clone.sunk | while | flops 551964672 | bytes 18970824 | solution.py:112
  225.1 2.3 fusion.101
  227.5 1.7 exponential_reduce_fusion.2
  229.7 2.4 fusion.101
  232.0 1.7 exponential_reduce_fusion.2
  234.2 2.4 fusion.101
  236.6 1.7 exponential_reduce_fusion.2
  238.7 2.3 fusion.101
  241.1 1.7 exponential_reduce_fusion.2
  242.8 23.8 %while.51 = (s32[]{:T(128)}, f32[256,4,4,128]{0,3,2,1:T(8,128)}, bf16[2048,4,128]{0,2,1:T(8,128)(2,1)}, s32[2048]{0:T(1024)S(1)}, s32[256]{0:T(256)S(1)}, /*inde...) while((s32[]{:T(128)}, f32[256,4,4,128]{0,3,2,1:T(8,128)}, ...), condition=%wide.region_11.12_spmd.clone, body=%wide.region_10.11_spmd.clone.sunk | while | flops 1083572224 | bytes 6586060 | solution.py:124
  243.2 5.0 %bitcast_add_fusion.4 = f32[256,4,4,128]{0,3,2,1:T(8,128)} fusion(f32[256,4,4,128]{0,3,2,1:T(8,128)} %get-tuple-element.1188, f32[4,4,256]{2,1,0:T(4,128)S(1)} %get-tuple-element.1210, pred[256,512]{0,1:T(8,128)(4,1)S(1)} %compare_and_fusion.7, bf16[256,4,4,128]{3,0,2,1:T(8,128)(2,1)S(1)} %get-tuple-element.1209, pred[]{:T(512)S(6)} %compare.35, ...), kind=kOutput, calls=%fused_computation.26.clone.1 | convolution fusion | flops 1083179008 | bytes 6440448 | tf_op jit(solution)/shard_map/while/body/eval_jaxpr/hgqk,khd->qhgd/dot_general | solution.py:120
  248.6 5.8 %bitcast_add_fusion.4 = f32[256,4,4,128]{0,3,2,1:T(8,128)} fusion(f32[256,4,4,128]{0,3,2,1:T(8,128)} %get-tuple-element.1188, f32[4,4,256]{2,1,0:T(4,128)S(1)} %get-tuple-element.1210, pred[256,512]{0,1:T(8,128)(4,1)S(1)} %compare_and_fusion.7, bf16[256,4,4,128]{3,0,2,1:T(8,128)(2,1)S(1)} %get-tuple-element.1209, pred[]{:T(512)S(6)} %compare.35, ...), kind=kOutput, calls=%fused_computation.26.clone.1 | convolution fusion | flops 1083179008 | bytes 6440448 | tf_op jit(solution)/shard_map/while/body/eval_jaxpr/hgqk,khd->qhgd/dot_general | solution.py:120
  254.8 5.8 %bitcast_add_fusion.4 = f32[256,4,4,128]{0,3,2,1:T(8,128)} fusion(f32[256,4,4,128]{0,3,2,1:T(8,128)} %get-tuple-element.1188, f32[4,4,256]{2,1,0:T(4,128)S(1)} %get-tuple-element.1210, pred[256,512]{0,1:T(8,128)(4,1)S(1)} %compare_and_fusion.7, bf16[256,4,4,128]{3,0,2,1:T(8,128)(2,1)S(1)} %get-tuple-element.1209, pred[]{:T(512)S(6)} %compare.35, ...), kind=kOutput, calls=%fused_computation.26.clone.1 | convolution fusion | flops 1083179008 | bytes 6440448 | tf_op jit(solution)/shard_map/while/body/eval_jaxpr/hgqk,khd->qhgd/dot_general | solution.py:120
  260.9 5.8 %bitcast_add_fusion.4 = f32[256,4,4,128]{0,3,2,1:T(8,128)} fusion(f32[256,4,4,128]{0,3,2,1:T(8,128)} %get-tuple-element.1188, f32[4,4,256]{2,1,0:T(4,128)S(1)} %get-tuple-element.1210, pred[256,512]{0,1:T(8,128)(4,1)S(1)} %compare_and_fusion.7, bf16[256,4,4,128]{3,0,2,1:T(8,128)(2,1)S(1)} %get-tuple-element.1209, pred[]{:T(512)S(6)} %compare.35, ...), kind=kOutput, calls=%fused_computation.26.clone.1 | convolution fusion | flops 1083179008 | bytes 6440448 | tf_op jit(solution)/shard_map/while/body/eval_jaxpr/hgqk,khd->qhgd/dot_general | solution.py:120
  266.6 2.1 multiply_reduce_fusion
  271.7 82.2 %while.52 = (s32[]{:T(128)}, f32[256,4,4,128]{0,3,2,1:T(8,128)S(1)}, bf16[2048,512]{1,0:T(8,128)(2,1)}, bf16[2048,512]{1,0:T(8,128)(2,1)}, bf16[2048,4,128]{2,0,...) while((s32[]{:T(128)}, ...), condition=%wide.region_14.15_spmd.clone, body=%wide.region_13.14_spmd.clone.sunk | while | flops 2707292160 | bytes 74381608 | solution.py:165
  272.3 2.7 fusion.117
  275.1 2.2 fusion.119
  277.3 5.3 %fusion.118 = bf16[4,4,256,512]{2,3,1,0:T(8,128)(2,1)} fusion(f32[4,512,256,4]{2,1,3,0:T(8,128)S(1)} %fusion.117, f32[4,4,256]{2,1,0:T(4,128)S(1)} %get-tuple-element.1264, f32[4,4,256]{2,1,0:T(4,128)S(1)} %get-tuple-element.1261, pred[256,512]{0,1:T(8,128)(4,1)S(1)} %compare_and_fusion.8, bf16[256,4,4,128]{0,3,2,1:T(8,128)(2,1)S(1)} %copy-done.3, ...), kind=kOutput, calls=%fused_computation.37.clone.1 | convolution fusion | flops 549453824 | bytes 14319620 | tf_op jit(solution)/shard_map/while/body/eval_jaxpr/qhgd,khd->hgqk/dot_general | solution.py:27
  282.9 4.9 fusion.120
  287.8 2.4 bitcast_add_fusion.5
  292.8 2.7 fusion.117
  295.6 2.3 fusion.119
  297.8 5.3 %fusion.118 = bf16[4,4,256,512]{2,3,1,0:T(8,128)(2,1)} fusion(f32[4,512,256,4]{2,1,3,0:T(8,128)S(1)} %fusion.117, f32[4,4,256]{2,1,0:T(4,128)S(1)} %get-tuple-element.1264, f32[4,4,256]{2,1,0:T(4,128)S(1)} %get-tuple-element.1261, pred[256,512]{0,1:T(8,128)(4,1)S(1)} %compare_and_fusion.8, bf16[256,4,4,128]{0,3,2,1:T(8,128)(2,1)S(1)} %copy-done.3, ...), kind=kOutput, calls=%fused_computation.37.clone.1 | convolution fusion | flops 549453824 | bytes 14319620 | tf_op jit(solution)/shard_map/while/body/eval_jaxpr/qhgd,khd->hgqk/dot_general | solution.py:27
  303.4 4.9 fusion.120
  308.3 2.4 bitcast_add_fusion.5
  313.3 2.7 fusion.117
  316.1 2.3 fusion.119
  318.3 5.3 %fusion.118 = bf16[4,4,256,512]{2,3,1,0:T(8,128)(2,1)} fusion(f32[4,512,256,4]{2,1,3,0:T(8,128)S(1)} %fusion.117, f32[4,4,256]{2,1,0:T(4,128)S(1)} %get-tuple-element.1264, f32[4,4,256]{2,1,0:T(4,128)S(1)} %get-tuple-element.1261, pred[256,512]{0,1:T(8,128)(4,1)S(1)} %compare_and_fusion.8, bf16[256,4,4,128]{0,3,2,1:T(8,128)(2,1)S(1)} %copy-done.3, ...), kind=kOutput, calls=%fused_computation.37.clone.1 | convolution fusion | flops 549453824 | bytes 14319620 | tf_op jit(solution)/shard_map/while/body/eval_jaxpr/qhgd,khd->hgqk/dot_general | solution.py:27
  323.9 4.9 fusion.120
  328.8 2.4 bitcast_add_fusion.5
  333.8 2.7 fusion.117
  336.6 2.3 fusion.119
  338.8 5.3 %fusion.118 = bf16[4,4,256,512]{2,3,1,0:T(8,128)(2,1)} fusion(f32[4,512,256,4]{2,1,3,0:T(8,128)S(1)} %fusion.117, f32[4,4,256]{2,1,0:T(4,128)S(1)} %get-tuple-element.1264, f32[4,4,256]{2,1,0:T(4,128)S(1)} %get-tuple-element.1261, pred[256,512]{0,1:T(8,128)(4,1)S(1)} %compare_and_fusion.8, bf16[256,4,4,128]{0,3,2,1:T(8,128)(2,1)S(1)} %copy-done.3, ...), kind=kOutput, calls=%fused_computation.37.clone.1 | convolution fusion | flops 549453824 | bytes 14319620 | tf_op jit(solution)/shard_map/while/body/eval_jaxpr/qhgd,khd->hgqk/dot_general | solution.py:27
  344.4 4.9 fusion.120
  349.3 2.4 bitcast_add_fusion.5
  354.0 4.7 pad_maximum_fusion
  358.6 6.4 %copy.114 = bf16[8,256,1024]{1,2,0:T(8,128)(2,1)} copy(bf16[8,256,1024]{2,1,0:T(8,128)(2,1)} %pad_maximum_fusion) | data formatting | bytes 8388608 | tf_op jit(solution)/shard_map/concatenate | solution.py:166
  365.1 4.7 all-to-all-start.1
  370.7 48.7 %all-to-all-done.1 = bf16[8,256,1024]{1,2,0:T(8,128)(2,1)} async-done(((bf16[8,256,1024]{1,2,0:T(8,128)(2,1)}), bf16[8,256,1024]{1,2,0:T(8,128)(2,1)}, u32[]{:S(2)}, u32[]{:S(2)}) %all-to-all-start.1) | async-done | bytes 4194336 | tf_op jit(solution)/shard_map/all_to_all | solution.py:168
  419.4 3.0 reduce_sum.45
  422.8 3.9 gather_fusion.1
  426.6 6.1 %reshape.360 = bf16[128,4,3072]{2,1,0:T(4,128)(2,1)} reshape(bf16[512,3072]{1,0:T(8,128)(2,1)} %gather_fusion.1) | data formatting | bytes 6291456 | tf_op jit(solution)/shard_map/reshape | solution.py:184
  432.8 7.5 %all-to-all-start.2 = ((bf16[128,4,3072]{2,1,0:T(4,128)(2,1)}), bf16[128,4,3072]{2,1,0:T(4,128)(2,1)}, u32[]{:S(2)}, u32[]{:S(2)}) async-start(bf16[128,4,3072]{2,1,0:T(4,128)(2,1)} %reshape.360), calls=%async_computation.2 | async-start | bytes 6291456 | tf_op jit(solution)/shard_map/all_to_all | solution.py:183
  440.3 40.9 %all-to-all-done.2 = bf16[128,4,3072]{2,1,0:T(4,128)(2,1)} async-done(((bf16[128,4,3072]{2,1,0:T(4,128)(2,1)}), bf16[128,4,3072]{2,1,0:T(4,128)(2,1)}, u32[]{:S(2)}, u32[]{:S(2)}) %all-to-all-start.2) | async-done | bytes 3145760 | tf_op jit(solution)/shard_map/all_to_all | solution.py:183
  481.2 4.5 reshape.361
  485.7 2.7 gather_fusion.2
  488.4 2.2 fusion.69
  (145 shorter events, 36.7 us)
Async XLA Ops:
  7.2 7.2 %copy-start.5 = (bf16[256,512]{1,0:T(8,128)(2,1)S(1)}, bf16[256,512]{1,0:T(8,128)(2,1)}, u32[]{:S(2)}) copy-start(bf16[256,512]{1,0:T(8,128)(2,1)} %param.18) | copy-start | bytes 786436
  7.2 7.9 %copy-start.6 = (bf16[256,512]{1,0:T(8,128)(2,1)S(1)}, bf16[256,512]{1,0:T(8,128)(2,1)}, u32[]{:S(2)}) copy-start(bf16[256,512]{1,0:T(8,128)(2,1)} %param.19) | copy-start | bytes 786436
  7.2 8.7 %copy-start.4 = (bf16[256,2048]{1,0:T(8,128)(2,1)S(1)}, bf16[256,2048]{1,0:T(8,128)(2,1)}, u32[]{:S(2)}) copy-start(bf16[256,2048]{1,0:T(8,128)(2,1)} %param.20) | copy-start | bytes 3145732
  11.9 5.6 %copy-start.8 = (s32[256]{0:T(256)}, s32[256]{0:T(256)S(1)}, u32[]{:S(2)}) copy-start(s32[256]{0:T(256)S(1)} %compare_select_fusion.4) | copy-start | bytes 3076
  35.6 12.5 %copy-start.10 = (s32[1,256]{1,0:T(1,128)S(1)}, s32[1,256]{1,0:T(1,128)}, u32[]{:S(2)}) copy-start(s32[1,256]{1,0:T(1,128)} %param.23) | copy-start | bytes 3076
  35.6 77.5 %all-to-all-start = ((bf16[128,4,5248]{2,1,0:T(4,128)(2,1)}), bf16[128,4,5248]{2,1,0:T(4,128)(2,1)}, u32[]{:S(2)}, u32[]{:S(2)}) async-start(bf16[128,4,5248]{2,1,0:T(4,128)(2,1)} %reshape.352), calls=%async_computation | async-start | bytes 10747904 | tf_op jit(solution)/shard_map/all_to_all | solution.py:53
  47.5 158.8 %all-gather.2.cloned.1.call-start = ((), (), s32[]{:S(2)}) async-start(), calls=%async_computation.3 | async-start | bytes 5308416 | tf_op jit(solution)/shard_map/all_gather | solution.py:77
  123.9 12.1 %copy-start.11 = (s32[1,16]{1,0:T(1,128)S(1)}, s32[1,16]{1,0:T(1,128)}, u32[]{:S(2)}) copy-start(s32[1,16]{1,0:T(1,128)} %param.22) | copy-start | bytes 196
  134.2 1.7 copy-start.2
  272.3 2.7 copy-start.3
  282.8 4.9 copy-start
  292.8 2.7 copy-start.3
  303.3 4.9 copy-start
  313.3 2.7 copy-start.3
  323.9 4.9 copy-start
  333.8 2.7 copy-start.3
  344.4 4.9 copy-start
  365.1 4.7 copy-start.7
  365.1 54.3 %all-to-all-start.1 = ((bf16[8,256,1024]{1,2,0:T(8,128)(2,1)}), bf16[8,256,1024]{1,2,0:T(8,128)(2,1)}, u32[]{:S(2)}, u32[]{:S(2)}) async-start(bf16[8,256,1024]{1,2,0:T(8,128)(2,1)} %copy.114), calls=%async_computation.1 | async-start | bytes 8388608 | tf_op jit(solution)/shard_map/all_to_all | solution.py:168
  432.8 7.5 %copy-start.9 = (s32[256]{0:T(256)S(1)}, s32[256]{0:T(256)}, u32[]{:S(2)}) copy-start(s32[256]{0:T(256)} %copy-done.8) | copy-start | bytes 3076
  432.8 48.4 %all-to-all-start.2 = ((bf16[128,4,3072]{2,1,0:T(4,128)(2,1)}), bf16[128,4,3072]{2,1,0:T(4,128)(2,1)}, u32[]{:S(2)}, u32[]{:S(2)}) async-start(bf16[128,4,3072]{2,1,0:T(4,128)(2,1)} %reshape.360), calls=%async_computation.2 | async-start | bytes 6291456 | tf_op jit(solution)/shard_map/all_to_all | solution.py:183
  488.4 2.3 copy-start.1
Sparse Core Ops, SparseCore 0:
  135.4 70.8 all-gather.1
where the time goes:
time: 508 us; the launch traced here: 499 us
  waiting for transfers between devices  213 us (42%)
  local copies, waits for them, and re-layouts  115 us (23%)
  matrix products  102 us (20%)
  other arithmetic  29 us (6%)
  starting transfers between devices  24.6 us (5%)
  between operations  14.6 us (3%)
    all_to_all x1, waiting for transfers between devices, local(): lax.all_to_all(holder.reshape(devices, capacity, width), ('dp', 'ctx'), s...  64.2 us
    all_gather x1, waiting for transfers between devices, local(): lax.all_gather(jnp.concatenate([kv_rows, doc_col], axis=1), 'ctx', axis=0...  59.6 us
    all_to_all x1, waiting for transfers between devices, local(): lax.all_to_all(partial.reshape(ctx_size, local_rows, 2 * k_cols), 'ctx',...  48.7 us
    all_to_all x1, waiting for transfers between devices, local(): lax.all_to_all(result[source_rows].reshape(devices, capacity, q_cols + 2...  40.9 us
    dot_general x4, matrix products, output_step(): jnp.einsum('hgqk,khd->qhgd', probs_low, value_blk, preferred_element_type...  22.3 us
    dot_general x4, matrix products, grad_terms(): jnp.einsum('qhgd,khd->hgqk', grad_blk, value_blk, preferred_element_type=...  21.3 us
    dot_general x8, matrix products, masked_scores(): jnp.einsum('qhgd,khd->hgqk', query_blk, key_blk, preferred_element_type=j...  20.3 us
    dot_general x4, matrix products, back_step(): jnp.einsum('hgqk,qhgd->khd', dscore_low, query_heads, preferred_element_t...  19.7 us
  transfers between devices with their start and end apart: 4, of which 4 were waited for; matrix products, arithmetic and copies ran while one was open for 2% of the time, Pallas kernels for 0%

commit v1 on v0

--- a/solution.py
+++ b/solution.py
@@ -74,9 +74,11 @@
     doc_col = (
         jnp.zeros((local_rows, 128), jnp.bfloat16).at[:, 0].set(doc_ids[0].astype(jnp.bfloat16))
     )
-    gathered = lax.all_gather(
-        jnp.concatenate([kv_rows, doc_col], axis=1), "ctx", axis=0, tiled=True
-    )
+    local_x = jnp.concatenate([kv_rows, doc_col], axis=1)
+    block_out = lax.axis_size("ctx")
+    e_now = jnp.stack(block_out * [local_x])
+    z_new = lax.all_to_all(e_now, axis_name="ctx", split_axis=0, concat_axis=0)
+    gathered = jnp.concatenate(z_new, axis=0)
     seq_docs = gathered[:, 2 * k_cols].astype(jnp.int32)
     doc_all = seq_docs.reshape(2 * ctx_size, span_rows)[span_seq].reshape(-1)
     own_docs = lax.dynamic_slice_in_dim(doc_all, ctx_index * local_rows, local_rows)

time: 508 us -> 479 us (0.943)
  waiting for transfers between devices: 213 us -> 196 us
  between operations: 14.6 us -> 1.21 us
    all_gather x1 -> x0, waiting for transfers between devices: 59.6 us -> none  [local(): lax.all_gather(jnp.concatenate([kv_rows, doc_col], axis=1), 'ctx', axis=0...]
    all_to_all x0 -> x1, waiting for transfers between devices: none -> 44.3 us  [local(): z_new = lax.all_to_all(e_now, axis_name='ctx', split_axis=0, concat_axis=0)]
    slice x2 -> x1, local copies, waits for them, and re-layouts: 8.49 us -> 2.29 us  [local(): value_heads = gathered[:, k_cols:2 * k_cols].reshape(pack_len, HK, DH)]
  transfers between devices with their start and end apart: 4 -> 4, of which waited for: 4 -> 4; matrix products, arithmetic and copies ran while one was open for 2% -> 3% of each run, Pallas kernels for 0% -> 0%
where the time goes in v1:
time: 479 us; the launch traced here: 470 us
  waiting for transfers between devices  196 us (41%)
  local copies, waits for them, and re-layouts  113 us (24%)
  matrix products  102 us (21%)
  starting transfers between devices  29.6 us (6%)
  other arithmetic  27.7 us (6%)
    all_to_all x1, waiting for transfers between devices, local(): lax.all_to_all(holder.reshape(devices, capacity, width), ('dp', 'ctx'), s...  64.5 us
    all_to_all x1, waiting for transfers between devices, local(): lax.all_to_all(partial.reshape(ctx_size, local_rows, 2 * k_cols), 'ctx',...  46.4 us
    all_to_all x1, waiting for transfers between devices, local(): z_new = lax.all_to_all(e_now, axis_name='ctx', split_axis=0, concat_axis=0)  44.3 us
    all_to_all x1, waiting for transfers between devices, local(): lax.all_to_all(result[source_rows].reshape(devices, capacity, q_cols + 2...  41 us
    dot_general x4, matrix products, output_step(): jnp.einsum('hgqk,khd->qhgd', probs_low, value_blk, preferred_element_type...  22.3 us
    dot_general x4, matrix products, grad_terms(): jnp.einsum('qhgd,khd->hgqk', grad_blk, value_blk, preferred_element_type=...  21.2 us
    dot_general x8, matrix products, masked_scores(): jnp.einsum('qhgd,khd->hgqk', query_blk, key_blk, preferred_element_type=j...  20.3 us
    dot_general x4, matrix products, back_step(): jnp.einsum('hgqk,qhgd->khd', dscore_low, query_heads, preferred_element_t...  19.7 us
  transfers between devices with their start and end apart: 4, of which 4 were waited for; matrix products, arithmetic and copies ran while one was open for 3% of the time, Pallas kernels for 0%

profile of v1, /device:TPU:1, one launch (start us, length us, event | category | flops | bytes accessed | tf_op | source)
XLA Modules:
  0.0 470.4 jit_solution(13478414303771620035)
XLA Ops:
  5.4 2.4 constant_dynamic-update-slice_fusion.5
  11.1 8.6 %scatter_custom_fusion = bf16[512,5248]{1,0:T(8,128)(2,1)} fusion(s32[256]{0:T(256)S(1)} %compare_select_fusion.4, bf16[256,5248]{1,0:T(8,128)(2,1)} %pad_dynamic-update-slice_fusion, bf16[]{:T(256)} %constant.226.clone.1), kind=kCustom, calls=%fused_computation.63 | custom fusion | bytes 5374464 | tf_op jit(solution)/shard_map/scatter | solution.py:52
  19.6 9.4 %reshape.357 = bf16[128,4,5248]{2,1,0:T(4,128)(2,1)} reshape(bf16[512,5248]{1,0:T(8,128)(2,1)} %scatter_custom_fusion) | data formatting | bytes 10747904 | tf_op jit(solution)/shard_map/reshape | solution.py:54
  29.1 12.6 %all-to-all-start = ((bf16[128,4,5248]{2,1,0:T(4,128)(2,1)}), bf16[128,4,5248]{2,1,0:T(4,128)(2,1)}, u32[]{:S(2)}, u32[]{:S(2)}) async-start(bf16[128,4,5248]{2,1,0:T(4,128)(2,1)} %reshape.357), calls=%async_computation | async-start | bytes 10747904 | tf_op jit(solution)/shard_map/all_to_all | solution.py:53
  42.5 64.5 %all-to-all-done = bf16[128,4,5248]{2,1,0:T(4,128)(2,1)} async-done(((bf16[128,4,5248]{2,1,0:T(4,128)(2,1)}), bf16[128,4,5248]{2,1,0:T(4,128)(2,1)}, u32[]{:S(2)}, u32[]{:S(2)}) %all-to-all-start) | async-done | bytes 5373984 | tf_op jit(solution)/shard_map/all_to_all | solution.py:53
  107.0 9.0 %reshape.405 = bf16[512,5248]{1,0:T(8,128)(2,1)} reshape(bf16[128,4,5248]{2,1,0:T(4,128)(2,1)} %all-to-all-done) | data formatting | bytes 10747904 | tf_op jit(solution)/shard_map/reshape | solution.py:59
  117.2 10.2 %scatter_custom_fusion.1 = bf16[256,5248]{1,0:T(8,128)(2,1)S(1)} fusion(s32[512]{0:T(512)S(1)} %get-tuple-element.848, bf16[512,5248]{1,0:T(8,128)(2,1)} %reshape.405, bf16[]{:T(256)} %constant.226.clone.1), kind=kCustom, calls=%fused_computation.68 | custom fusion | bytes 2687488 | tf_op jit(solution)/shard_map/scatter | solution.py:62
  128.8 3.5 stack.2
  132.4 4.9 %all-to-all-start.1 = ((bf16[8,256,1152]{1,2,0:T(8,128)(2,1)}), bf16[8,256,1152]{1,2,0:T(8,128)(2,1)}, u32[]{:S(2)}, u32[]{:S(2)}) async-start(bf16[8,256,1152]{1,2,0:T(8,128)(2,1)} %stack.2), calls=%async_computation.1 | async-start | bytes 9437184 | tf_op jit(solution)/shard_map/all_to_all | solution.py:80
  137.5 2.8 fusion.68
  143.3 2.4 copy.106
  145.7 2.3 copy.132
  148.6 44.3 %all-to-all-done.1 = bf16[8,256,1152]{1,2,0:T(8,128)(2,1)} async-done(((bf16[8,256,1152]{1,2,0:T(8,128)(2,1)}), bf16[8,256,1152]{1,2,0:T(8,128)(2,1)}, u32[]{:S(2)}, u32[]{:S(2)}) %all-to-all-start.1) | async-done | bytes 4718624 | tf_op jit(solution)/shard_map/all_to_all | solution.py:80
  192.9 3.0 copy.141
  195.9 2.3 fusion.67
  198.2 4.0 copy.105
  202.8 18.0 %while.50 = (s32[]{:T(128)}, f32[4,4,256]{2,1,0:T(4,128)S(1)}, f32[4,4,256]{2,1,0:T(4,128)S(1)}, s32[2048]{0:T(1024)S(1)}, s32[256]{0:T(256)S(1)}, /*index=5*/s3...) while((s32[]{:T(128)}, f32[4,4,256]{2,1,0:T(4,128)S(1)}, ...), condition=%wide.region_9.10_spmd.clone, body=%wide.region_6.9_spmd.clone.sunk | while | flops 551964672 | bytes 18970824 | solution.py:114
  203.2 2.3 fusion.101
  205.6 1.7 exponential_reduce_fusion.2
  207.7 2.4 fusion.101
  210.1 1.7 exponential_reduce_fusion.2
  212.2 2.4 fusion.101
  214.6 1.7 exponential_reduce_fusion.2
  216.7 2.3 fusion.101
  219.1 1.7 exponential_reduce_fusion.2
  220.9 23.8 %while.51 = (s32[]{:T(128)}, f32[256,4,4,128]{0,3,2,1:T(8,128)}, bf16[2048,4,128]{0,2,1:T(8,128)(2,1)}, s32[2048]{0:T(1024)S(1)}, s32[256]{0:T(256)S(1)}, /*inde...) while((s32[]{:T(128)}, f32[256,4,4,128]{0,3,2,1:T(8,128)}, ...), condition=%wide.region_11.12_spmd.clone, body=%wide.region_10.11_spmd.clone.sunk | while | flops 1083572224 | bytes 6586060 | solution.py:126
  221.3 5.0 %bitcast_add_fusion.4 = f32[256,4,4,128]{0,3,2,1:T(8,128)} fusion(f32[256,4,4,128]{0,3,2,1:T(8,128)} %get-tuple-element.1190, f32[4,4,256]{2,1,0:T(4,128)S(1)} %get-tuple-element.1212, pred[256,512]{0,1:T(8,128)(4,1)S(1)} %compare_and_fusion.7, bf16[256,4,4,128]{3,0,2,1:T(8,128)(2,1)S(1)} %get-tuple-element.1211, pred[]{:T(512)S(6)} %compare.35, ...), kind=kOutput, calls=%fused_computation.26.clone.1 | convolution fusion | flops 1083179008 | bytes 6440448 | tf_op jit(solution)/shard_map/while/body/eval_jaxpr/hgqk,khd->qhgd/dot_general | solution.py:122
  226.7 5.8 %bitcast_add_fusion.4 = f32[256,4,4,128]{0,3,2,1:T(8,128)} fusion(f32[256,4,4,128]{0,3,2,1:T(8,128)} %get-tuple-element.1190, f32[4,4,256]{2,1,0:T(4,128)S(1)} %get-tuple-element.1212, pred[256,512]{0,1:T(8,128)(4,1)S(1)} %compare_and_fusion.7, bf16[256,4,4,128]{3,0,2,1:T(8,128)(2,1)S(1)} %get-tuple-element.1211, pred[]{:T(512)S(6)} %compare.35, ...), kind=kOutput, calls=%fused_computation.26.clone.1 | convolution fusion | flops 1083179008 | bytes 6440448 | tf_op jit(solution)/shard_map/while/body/eval_jaxpr/hgqk,khd->qhgd/dot_general | solution.py:122
  232.8 5.8 %bitcast_add_fusion.4 = f32[256,4,4,128]{0,3,2,1:T(8,128)} fusion(f32[256,4,4,128]{0,3,2,1:T(8,128)} %get-tuple-element.1190, f32[4,4,256]{2,1,0:T(4,128)S(1)} %get-tuple-element.1212, pred[256,512]{0,1:T(8,128)(4,1)S(1)} %compare_and_fusion.7, bf16[256,4,4,128]{3,0,2,1:T(8,128)(2,1)S(1)} %get-tuple-element.1211, pred[]{:T(512)S(6)} %compare.35, ...), kind=kOutput, calls=%fused_computation.26.clone.1 | convolution fusion | flops 1083179008 | bytes 6440448 | tf_op jit(solution)/shard_map/while/body/eval_jaxpr/hgqk,khd->qhgd/dot_general | solution.py:122
  238.9 5.8 %bitcast_add_fusion.4 = f32[256,4,4,128]{0,3,2,1:T(8,128)} fusion(f32[256,4,4,128]{0,3,2,1:T(8,128)} %get-tuple-element.1190, f32[4,4,256]{2,1,0:T(4,128)S(1)} %get-tuple-element.1212, pred[256,512]{0,1:T(8,128)(4,1)S(1)} %compare_and_fusion.7, bf16[256,4,4,128]{3,0,2,1:T(8,128)(2,1)S(1)} %get-tuple-element.1211, pred[]{:T(512)S(6)} %compare.35, ...), kind=kOutput, calls=%fused_computation.26.clone.1 | convolution fusion | flops 1083179008 | bytes 6440448 | tf_op jit(solution)/shard_map/while/body/eval_jaxpr/hgqk,khd->qhgd/dot_general | solution.py:122
  244.7 2.1 multiply_reduce_fusion
  249.8 82.1 %while.52 = (s32[]{:T(128)}, f32[256,4,4,128]{0,3,2,1:T(8,128)S(1)}, bf16[2048,512]{1,0:T(8,128)(2,1)}, bf16[2048,512]{1,0:T(8,128)(2,1)}, bf16[2048,4,128]{2,0,...) while((s32[]{:T(128)}, ...), condition=%wide.region_14.15_spmd.clone, body=%wide.region_13.14_spmd.clone.sunk | while | flops 2707292160 | bytes 74381608 | solution.py:167
  250.4 2.7 fusion.117
  253.1 2.2 fusion.119
  255.4 5.3 %fusion.118 = bf16[4,4,256,512]{2,3,1,0:T(8,128)(2,1)} fusion(f32[4,512,256,4]{2,1,3,0:T(8,128)S(1)} %fusion.117, f32[4,4,256]{2,1,0:T(4,128)S(1)} %get-tuple-element.1266, f32[4,4,256]{2,1,0:T(4,128)S(1)} %get-tuple-element.1263, pred[256,512]{0,1:T(8,128)(4,1)S(1)} %compare_and_fusion.8, bf16[256,4,4,128]{0,3,2,1:T(8,128)(2,1)S(1)} %copy-done.3, ...), kind=kOutput, calls=%fused_computation.37.clone.1 | convolution fusion | flops 549453824 | bytes 14319620 | tf_op jit(solution)/shard_map/while/body/eval_jaxpr/qhgd,khd->hgqk/dot_general | solution.py:27
  260.9 4.9 %fusion.120 = bf16[4,512,128]{1,2,0:T(8,128)(2,1)} fusion(bf16[4,4,256,512]{2,3,1,0:T(8,128)(2,1)} %fusion.118, bf16[256,4,4,128]{0,3,2,1:T(8,128)(2,1)} %get-tuple-element.1262), kind=kOutput, calls=%fused_computation.46.clone.1 | convolution fusion | flops 537395200 | bytes 5767168 | tf_op jit(solution)/shard_map/while/body/eval_jaxpr/hgqk,qhgd->khd/dot_general | solution.py:145
  265.8 2.4 bitcast_add_fusion.5
  270.9 2.7 fusion.117
  273.6 2.3 fusion.119
  275.9 5.3 %fusion.118 = bf16[4,4,256,512]{2,3,1,0:T(8,128)(2,1)} fusion(f32[4,512,256,4]{2,1,3,0:T(8,128)S(1)} %fusion.117, f32[4,4,256]{2,1,0:T(4,128)S(1)} %get-tuple-element.1266, f32[4,4,256]{2,1,0:T(4,128)S(1)} %get-tuple-element.1263, pred[256,512]{0,1:T(8,128)(4,1)S(1)} %compare_and_fusion.8, bf16[256,4,4,128]{0,3,2,1:T(8,128)(2,1)S(1)} %copy-done.3, ...), kind=kOutput, calls=%fused_computation.37.clone.1 | convolution fusion | flops 549453824 | bytes 14319620 | tf_op jit(solution)/shard_map/while/body/eval_jaxpr/qhgd,khd->hgqk/dot_general | solution.py:27
  281.4 4.9 %fusion.120 = bf16[4,512,128]{1,2,0:T(8,128)(2,1)} fusion(bf16[4,4,256,512]{2,3,1,0:T(8,128)(2,1)} %fusion.118, bf16[256,4,4,128]{0,3,2,1:T(8,128)(2,1)} %get-tuple-element.1262), kind=kOutput, calls=%fused_computation.46.clone.1 | convolution fusion | flops 537395200 | bytes 5767168 | tf_op jit(solution)/shard_map/while/body/eval_jaxpr/hgqk,qhgd->khd/dot_general | solution.py:145
  286.3 2.4 bitcast_add_fusion.5
  291.3 2.7 fusion.117
  294.1 2.3 fusion.119
  296.3 5.3 %fusion.118 = bf16[4,4,256,512]{2,3,1,0:T(8,128)(2,1)} fusion(f32[4,512,256,4]{2,1,3,0:T(8,128)S(1)} %fusion.117, f32[4,4,256]{2,1,0:T(4,128)S(1)} %get-tuple-element.1266, f32[4,4,256]{2,1,0:T(4,128)S(1)} %get-tuple-element.1263, pred[256,512]{0,1:T(8,128)(4,1)S(1)} %compare_and_fusion.8, bf16[256,4,4,128]{0,3,2,1:T(8,128)(2,1)S(1)} %copy-done.3, ...), kind=kOutput, calls=%fused_computation.37.clone.1 | convolution fusion | flops 549453824 | bytes 14319620 | tf_op jit(solution)/shard_map/while/body/eval_jaxpr/qhgd,khd->hgqk/dot_general | solution.py:27
  301.8 4.9 %fusion.120 = bf16[4,512,128]{1,2,0:T(8,128)(2,1)} fusion(bf16[4,4,256,512]{2,3,1,0:T(8,128)(2,1)} %fusion.118, bf16[256,4,4,128]{0,3,2,1:T(8,128)(2,1)} %get-tuple-element.1262), kind=kOutput, calls=%fused_computation.46.clone.1 | convolution fusion | flops 537395200 | bytes 5767168 | tf_op jit(solution)/shard_map/while/body/eval_jaxpr/hgqk,qhgd->khd/dot_general | solution.py:145
  306.8 2.4 bitcast_add_fusion.5
  311.8 2.7 fusion.117
  314.6 2.3 fusion.119
  316.8 5.3 %fusion.118 = bf16[4,4,256,512]{2,3,1,0:T(8,128)(2,1)} fusion(f32[4,512,256,4]{2,1,3,0:T(8,128)S(1)} %fusion.117, f32[4,4,256]{2,1,0:T(4,128)S(1)} %get-tuple-element.1266, f32[4,4,256]{2,1,0:T(4,128)S(1)} %get-tuple-element.1263, pred[256,512]{0,1:T(8,128)(4,1)S(1)} %compare_and_fusion.8, bf16[256,4,4,128]{0,3,2,1:T(8,128)(2,1)S(1)} %copy-done.3, ...), kind=kOutput, calls=%fused_computation.37.clone.1 | convolution fusion | flops 549453824 | bytes 14319620 | tf_op jit(solution)/shard_map/while/body/eval_jaxpr/qhgd,khd->hgqk/dot_general | solution.py:27
  322.3 4.9 %fusion.120 = bf16[4,512,128]{1,2,0:T(8,128)(2,1)} fusion(bf16[4,4,256,512]{2,3,1,0:T(8,128)(2,1)} %fusion.118, bf16[256,4,4,128]{0,3,2,1:T(8,128)(2,1)} %get-tuple-element.1262), kind=kOutput, calls=%fused_computation.46.clone.1 | convolution fusion | flops 537395200 | bytes 5767168 | tf_op jit(solution)/shard_map/while/body/eval_jaxpr/hgqk,qhgd->khd/dot_general | solution.py:145
  327.2 2.4 bitcast_add_fusion.5
  331.9 4.7 pad_maximum_fusion
  336.6 6.4 %copy.112 = bf16[8,256,1024]{1,2,0:T(8,128)(2,1)} copy(bf16[8,256,1024]{2,1,0:T(8,128)(2,1)} %pad_maximum_fusion) | data formatting | bytes 8388608 | tf_op jit(solution)/shard_map/concatenate | solution.py:168
  343.1 4.5 all-to-all-start.2
  350.3 46.4 %all-to-all-done.2 = bf16[8,256,1024]{1,2,0:T(8,128)(2,1)} async-done(((bf16[8,256,1024]{1,2,0:T(8,128)(2,1)}), bf16[8,256,1024]{1,2,0:T(8,128)(2,1)}, u32[]{:S(2)}, u32[]{:S(2)}) %all-to-all-start.2) | async-done | bytes 4194336 | tf_op jit(solution)/shard_map/all_to_all | solution.py:170
  396.8 3.0 reduce_sum.45
  400.5 3.8 gather_fusion.1
  404.4 6.1 %reshape.366 = bf16[128,4,3072]{2,1,0:T(4,128)(2,1)} reshape(bf16[512,3072]{1,0:T(8,128)(2,1)} %gather_fusion.1) | data formatting | bytes 6291456 | tf_op jit(solution)/shard_map/reshape | solution.py:186
  410.5 7.6 %all-to-all-start.3 = ((bf16[128,4,3072]{2,1,0:T(4,128)(2,1)}), bf16[128,4,3072]{2,1,0:T(4,128)(2,1)}, u32[]{:S(2)}, u32[]{:S(2)}) async-start(bf16[128,4,3072]{2,1,0:T(4,128)(2,1)} %reshape.366), calls=%async_computation.3 | async-start | bytes 6291456 | tf_op jit(solution)/shard_map/all_to_all | solution.py:185
  418.1 41.0 %all-to-all-done.3 = bf16[128,4,3072]{2,1,0:T(4,128)(2,1)} async-done(((bf16[128,4,3072]{2,1,0:T(4,128)(2,1)}), bf16[128,4,3072]{2,1,0:T(4,128)(2,1)}, u32[]{:S(2)}, u32[]{:S(2)}) %all-to-all-start.3) | async-done | bytes 3145760 | tf_op jit(solution)/shard_map/all_to_all | solution.py:185
  459.1 4.5 reshape.367
  463.6 2.7 gather_fusion.2
  466.3 2.2 fusion.69
  (144 shorter events, 38.3 us)
Async XLA Ops:
  0.6 7.2 %copy-start.5 = (bf16[256,512]{1,0:T(8,128)(2,1)S(1)}, bf16[256,512]{1,0:T(8,128)(2,1)}, u32[]{:S(2)}) copy-start(bf16[256,512]{1,0:T(8,128)(2,1)} %param.18) | copy-start | bytes 786436
  0.6 7.9 %copy-start.6 = (bf16[256,512]{1,0:T(8,128)(2,1)S(1)}, bf16[256,512]{1,0:T(8,128)(2,1)}, u32[]{:S(2)}) copy-start(bf16[256,512]{1,0:T(8,128)(2,1)} %param.19) | copy-start | bytes 786436
  0.7 8.7 %copy-start.4 = (bf16[256,2048]{1,0:T(8,128)(2,1)S(1)}, bf16[256,2048]{1,0:T(8,128)(2,1)}, u32[]{:S(2)}) copy-start(bf16[256,2048]{1,0:T(8,128)(2,1)} %param.20) | copy-start | bytes 3145732
  5.4 5.6 %copy-start.8 = (s32[256]{0:T(256)}, s32[256]{0:T(256)S(1)}, u32[]{:S(2)}) copy-start(s32[256]{0:T(256)S(1)} %compare_select_fusion.4) | copy-start | bytes 3076
  29.1 12.6 %copy-start.10 = (s32[1,256]{1,0:T(1,128)S(1)}, s32[1,256]{1,0:T(1,128)}, u32[]{:S(2)}) copy-start(s32[1,256]{1,0:T(1,128)} %param.23) | copy-start | bytes 3076
  29.1 77.9 %all-to-all-start = ((bf16[128,4,5248]{2,1,0:T(4,128)(2,1)}), bf16[128,4,5248]{2,1,0:T(4,128)(2,1)}, u32[]{:S(2)}, u32[]{:S(2)}) async-start(bf16[128,4,5248]{2,1,0:T(4,128)(2,1)} %reshape.357), calls=%async_computation | async-start | bytes 10747904 | tf_op jit(solution)/shard_map/all_to_all | solution.py:53
  127.3 5.0 %copy-start.2 = (bf16[256,5248]{1,0:T(8,128)(2,1)}, bf16[256,5248]{1,0:T(8,128)(2,1)S(1)}, u32[]{:S(2)}) copy-start(bf16[256,5248]{1,0:T(8,128)(2,1)S(1)} %scatter_custom_fusion.1) | copy-start | bytes 8060932
  132.4 4.9 %copy-start.11 = (s32[1,16]{1,0:T(1,128)S(1)}, s32[1,16]{1,0:T(1,128)}, u32[]{:S(2)}) copy-start(s32[1,16]{1,0:T(1,128)} %param.22) | copy-start | bytes 196
  132.4 60.6 %all-to-all-start.1 = ((bf16[8,256,1152]{1,2,0:T(8,128)(2,1)}), bf16[8,256,1152]{1,2,0:T(8,128)(2,1)}, u32[]{:S(2)}, u32[]{:S(2)}) async-start(bf16[8,256,1152]{1,2,0:T(8,128)(2,1)} %stack.2), calls=%async_computation.1 | async-start | bytes 9437184 | tf_op jit(solution)/shard_map/all_to_all | solution.py:80
  250.4 2.7 copy-start.3
  260.9 4.9 %copy-start = (bf16[4,4,256,512]{2,3,1,0:T(8,128)(2,1)S(1)}, bf16[4,4,256,512]{2,3,1,0:T(8,128)(2,1)}, u32[]{:S(2)}) copy-start(bf16[4,4,256,512]{2,3,1,0:T(8,128)(2,1)} %fusion.118) | copy-start | bytes 12582916 | tf_op jit(solution)/shard_map/while
  270.9 2.7 copy-start.3
  281.4 4.9 %copy-start = (bf16[4,4,256,512]{2,3,1,0:T(8,128)(2,1)S(1)}, bf16[4,4,256,512]{2,3,1,0:T(8,128)(2,1)}, u32[]{:S(2)}) copy-start(bf16[4,4,256,512]{2,3,1,0:T(8,128)(2,1)} %fusion.118) | copy-start | bytes 12582916 | tf_op jit(solution)/shard_map/while
  291.3 2.7 copy-start.3
  301.8 4.9 %copy-start = (bf16[4,4,256,512]{2,3,1,0:T(8,128)(2,1)S(1)}, bf16[4,4,256,512]{2,3,1,0:T(8,128)(2,1)}, u32[]{:S(2)}) copy-start(bf16[4,4,256,512]{2,3,1,0:T(8,128)(2,1)} %fusion.118) | copy-start | bytes 12582916 | tf_op jit(solution)/shard_map/while
  311.8 2.7 copy-start.3
  322.3 4.9 %copy-start = (bf16[4,4,256,512]{2,3,1,0:T(8,128)(2,1)S(1)}, bf16[4,4,256,512]{2,3,1,0:T(8,128)(2,1)}, u32[]{:S(2)}) copy-start(bf16[4,4,256,512]{2,3,1,0:T(8,128)(2,1)} %fusion.118) | copy-start | bytes 12582916 | tf_op jit(solution)/shard_map/while
  343.1 53.7 %all-to-all-start.2 = ((bf16[8,256,1024]{1,2,0:T(8,128)(2,1)}), bf16[8,256,1024]{1,2,0:T(8,128)(2,1)}, u32[]{:S(2)}, u32[]{:S(2)}) async-start(bf16[8,256,1024]{1,2,0:T(8,128)(2,1)} %copy.112), calls=%async_computation.2 | async-start | bytes 8388608 | tf_op jit(solution)/shard_map/all_to_all | solution.py:170
  399.8 0.7 copy-start.7
  410.5 7.6 %copy-start.9 = (s32[256]{0:T(256)S(1)}, s32[256]{0:T(256)}, u32[]{:S(2)}) copy-start(s32[256]{0:T(256)} %copy-done.8) | copy-start | bytes 3076
  410.5 48.7 %all-to-all-start.3 = ((bf16[128,4,3072]{2,1,0:T(4,128)(2,1)}), bf16[128,4,3072]{2,1,0:T(4,128)(2,1)}, u32[]{:S(2)}, u32[]{:S(2)}) async-start(bf16[128,4,3072]{2,1,0:T(4,128)(2,1)} %reshape.366), calls=%async_computation.3 | async-start | bytes 6291456 | tf_op jit(solution)/shard_map/all_to_all | solution.py:185
  466.3 2.3 copy-start.1
